TPU v7x, 128 devices: a whole 4x4x4 slice. The times are simulated.
128 devices in a mesh: dp: 16 (over x, z), fsdp: 8 (over y, core).
Axes of the slice: x: 4, y: 4, z: 4, core: 2. Of those that a mesh axis runs over, the one named last changes fastest.
Arguments:
- tokens: bfloat16 [2048, 4096], P('dp', 'fsdp'), may hold values from -6 to 6
- expert_ids: int32 [2048, 2], P('dp'), may hold values from 0 to 7, all different within a row; in each aligned block of 128 rows (0 to 127, 128 to 255, ...) at most 40 rows name the same one
- route_probs: float32 [2048, 2], P('dp'), may hold values from 0.1 to 0.9
- w_gate: bfloat16 [4096, 65536], P(None, ('dp', 'fsdp')), may hold values from -0.09375 to 0.09375
- w_up: bfloat16 [4096, 65536], P(None, ('dp', 'fsdp')), may hold values from -0.09375 to 0.09375
- w_down: bfloat16 [65536, 4096], P(('dp', 'fsdp')), may hold values from -0.0625 to 0.0625
- out_grad: bfloat16 [2048, 4096], P('dp', 'fsdp'), may hold values from -0.59765625 to 0.59765625
Outputs:
- mixed: bfloat16 [2048, 4096], P('dp', 'fsdp')
- token_grad: bfloat16 [2048, 4096], P('dp', 'fsdp')
- prob_grad: float32 [2048, 2], P('dp')
- gate_weight_grad: bfloat16 [4096, 65536], P(None, ('dp', 'fsdp'))
- up_weight_grad: bfloat16 [4096, 65536], P(None, ('dp', 'fsdp'))
- down_weight_grad: bfloat16 [65536, 4096], P(('dp', 'fsdp'))
Inputs may be any that keep to these rules, and one draw needn't show every extreme that they name: `expert_ids`: each token names two different experts. Within the 128 tokens of one dp index (aligned blocks of rows) no expert is named more than 40 times, and in some block one expert is named exactly 40 times.
All inputs are finite; a program needn't handle non-finite values.
Results may differ from a plain program's by a relative error of at most 0.019.
Values may be sent and summed in bfloat16 or wider, within the bound.
No kernel may reach another device: no remote copies, remote signals or barrier semaphores. Data moves between devices by JAX's collectives and lax.ppermute only.
A program may use at most 128 MiB of HBM per device.

v0:
```python
import jax
import jax.numpy as jnp
from jax import lax
from jax.sharding import PartitionSpec as P

E = 8
CAP = 40


def local(tokens, expert_ids, route_probs, w_gate, w_up, w_down, out_grad):
    dp_count = lax.axis_size("dp")
    groups = dp_count // E
    token_count = tokens.shape[0]
    slot_total = E * CAP
    routing = expert_ids.reshape(-1)
    onehot = (routing[:, None] == jnp.arange(E, dtype=jnp.int32)[None, :]).astype(jnp.int32)
    position = jnp.sum((jnp.cumsum(onehot, axis=0) - onehot) * onehot, axis=1)
    slot_of = (routing * CAP + position).reshape(token_count, 2)
    slot_index = jnp.arange(slot_total, dtype=jnp.int32)
    select_first = slot_of[:, 0:1] == slot_index[None, :]
    select_second = slot_of[:, 1:2] == slot_index[None, :]
    picker = jnp.logical_or(select_first, select_second)
    picker_bf = picker.astype(jnp.bfloat16)
    weighted = jnp.where(select_first, route_probs[:, 0:1], 0.0) + jnp.where(
        select_second, route_probs[:, 1:2], 0.0
    )
    contract_rows = (((0,), (0,)), ((), ()))
    back_dims = (((1,), (1,)), ((), ()))

    def place_rows(source, scaled):
        if scaled:
            placed = lax.dot_general(
                weighted,
                source.astype(jnp.float32),
                contract_rows,
                precision=lax.Precision.HIGHEST,
                preferred_element_type=jnp.float32,
            )
        else:
            placed = lax.dot_general(
                picker_bf, source, contract_rows, preferred_element_type=jnp.float32
            )
        placed = placed.astype(jnp.bfloat16).reshape(E, CAP, source.shape[1])
        return jnp.repeat(placed, groups, axis=0)

    def to_expert_layout(source, scaled):
        joined = lax.all_gather(source, "fsdp", axis=1, tiled=True)
        arrived = lax.all_to_all(
            place_rows(joined, scaled), "dp", split_axis=0, concat_axis=0, tiled=True
        )
        return arrived.reshape(dp_count * CAP, arrived.shape[2])

    def to_token_layout(partial_value):
        shares = lax.psum_scatter(
            partial_value.astype(jnp.bfloat16), "fsdp", scatter_dimension=1, tiled=True
        ).astype(jnp.float32)
        returned = lax.all_to_all(
            shares.reshape(dp_count, CAP, shares.shape[1]).astype(jnp.bfloat16),
            "dp",
            split_axis=0,
            concat_axis=0,
            tiled=True,
        ).astype(jnp.float32)
        return jnp.sum(returned.reshape(E, groups, CAP, returned.shape[2]), axis=1).reshape(
            slot_total, returned.shape[2]
        )

    expert_rows = to_expert_layout(tokens, False)
    gate_proj = jnp.dot(expert_rows, w_gate, preferred_element_type=jnp.float32)
    up_proj = jnp.dot(expert_rows, w_up, preferred_element_type=jnp.float32)
    sigmoid_gate = jax.nn.sigmoid(gate_proj)
    activated = gate_proj * sigmoid_gate
    hidden = (activated * up_proj).astype(jnp.bfloat16)
    out_partial = jnp.dot(hidden, w_down, preferred_element_type=jnp.float32)
    out_slots = to_token_layout(out_partial)
    first_pair = jnp.dot(
        select_first.astype(jnp.float32),
        out_slots,
        precision=lax.Precision.HIGHEST,
        preferred_element_type=jnp.float32,
    )
    second_pair = jnp.dot(
        select_second.astype(jnp.float32),
        out_slots,
        precision=lax.Precision.HIGHEST,
        preferred_element_type=jnp.float32,
    )
    mixed = (route_probs[:, 0:1] * first_pair + route_probs[:, 1:2] * second_pair).astype(
        jnp.bfloat16
    )
    grad_local = out_grad.astype(jnp.float32)
    prob_terms = jnp.stack(
        [jnp.sum(first_pair * grad_local, axis=1), jnp.sum(second_pair * grad_local, axis=1)],
        axis=1,
    )
    prob_grad = lax.psum(prob_terms, "fsdp")
    grad_rows = to_expert_layout(out_grad, True)
    hidden_grad = lax.dot_general(grad_rows, w_down, back_dims, preferred_element_type=jnp.float32)
    gate_grad = (
        hidden_grad * up_proj * sigmoid_gate * (1.0 + gate_proj * (1.0 - sigmoid_gate))
    ).astype(jnp.bfloat16)
    up_grad = (hidden_grad * activated).astype(jnp.bfloat16)
    gate_weight_grad = lax.dot_general(
        expert_rows, gate_grad, contract_rows, preferred_element_type=jnp.float32
    ).astype(jnp.bfloat16)
    up_weight_grad = lax.dot_general(
        expert_rows, up_grad, contract_rows, preferred_element_type=jnp.float32
    ).astype(jnp.bfloat16)
    down_weight_grad = lax.dot_general(
        hidden, grad_rows, contract_rows, preferred_element_type=jnp.float32
    ).astype(jnp.bfloat16)
    input_partial = lax.dot_general(
        gate_grad, w_gate, back_dims, preferred_element_type=jnp.float32
    )
    input_partial = input_partial + lax.dot_general(
        up_grad, w_up, back_dims, preferred_element_type=jnp.float32
    )
    input_slots = to_token_layout(input_partial)
    token_grad = jnp.dot(
        picker.astype(jnp.float32),
        input_slots,
        precision=lax.Precision.HIGHEST,
        preferred_element_type=jnp.float32,
    ).astype(jnp.bfloat16)
    return (mixed, token_grad, prob_grad, gate_weight_grad, up_weight_grad, down_weight_grad)


def solution(mesh):
    placed = (
        P("dp", "fsdp"),
        P("dp", None),
        P("dp", None),
        P(None, ("dp", "fsdp")),
        P(None, ("dp", "fsdp")),
        P(("dp", "fsdp"), None),
        P("dp", "fsdp"),
    )
    return jax.shard_map(
        local,
        mesh=mesh,
        in_specs=placed,
        out_specs=(
            P("dp", "fsdp"),
            P("dp", "fsdp"),
            P("dp", None),
            P(None, ("dp", "fsdp")),
            P(None, ("dp", "fsdp")),
            P(("dp", "fsdp"), None),
        ),
        check_vma=False,
    )
```

profile of v0, /device:TPU:2, one launch (start us, length us, event | category | flops | bytes accessed | tf_op | source)
XLA Modules:
  0.0 347.4 jit_solution(6366988755404527250)
XLA Ops:
  10.8 24.6 %all-gather.3.cloned.1.call-done = bf16[128,4096]{1,0:T(8,128)(2,1)} async-done(((bf16[128,512]{1,0:T(8,128)(2,1)}), bf16[128,4096]{1,0:T(8,128)(2,1)}) %all-gather.3.cloned.1.call-update) | async-done | bytes 1048592 | tf_op jit(solution)/shard_map/all_gather | solution.py:47
  35.5 2.2 convolution_convert_fusion.5
  37.6 3.0 broadcast_in_dim.27
  40.6 7.5 %all-to-all-start = ((bf16[16,40,4096]{2,1,0:T(8,128)(2,1)}), bf16[16,40,4096]{2,1,0:T(8,128)(2,1)}, u32[]{:S(2)}, u32[]{:S(2)}) async-start(bf16[16,40,4096]{2,1,0:T(8,128)(2,1)} %bitcast.57), calls=%async_computation | async-start | bytes 10485760 | tf_op jit(solution)/shard_map/all_to_all | solution.py:48
  49.0 24.8 %all-gather.5.cloned.1.call-done = bf16[128,4096]{1,0:T(8,128)(2,1)} async-done(((bf16[128,512]{1,0:T(8,128)(2,1)}), bf16[128,4096]{1,0:T(8,128)(2,1)}) %all-gather.5.cloned.1.call-update) | async-done | bytes 1048592 | tf_op jit(solution)/shard_map/all_gather | solution.py:47
  73.8 3.6 %convolution_convert_fusion.4 = bf16[320,4096]{1,0:T(8,128)(2,1)S(1)} fusion(bf16[128,4096]{1,0:T(8,128)(2,1)} %all-gather.5.cloned.1.call-done, f32[128]{0:T(128)S(1)} %get-tuple-element.13, f32[128]{0:T(128)S(1)} %get-tuple-element.12, s32[128]{0:T(128)S(1)} %get-tuple-element.15, s32[128]{0:T(128)S(1)} %get-tuple-element.14), kind=kOutput, calls=%fused_computation.5 | convolution fusion | flops 2014781440 | bytes 3672064 | tf_op jit(solution)/shard_map/dot_general | solution.py:32
  77.4 38.4 %all-to-all-done = bf16[16,40,4096]{2,1,0:T(8,128)(2,1)} async-done(((bf16[16,40,4096]{2,1,0:T(8,128)(2,1)}), bf16[16,40,4096]{2,1,0:T(8,128)(2,1)}, u32[]{:S(2)}, u32[]{:S(2)}) %all-to-all-start) | async-done | bytes 5242912 | tf_op jit(solution)/shard_map/all_to_all | solution.py:48
  115.7 3.0 broadcast_in_dim.31
  118.7 24.0 %all-to-all-start.2 = ((bf16[16,40,4096]{2,1,0:T(8,128)(2,1)}), bf16[16,40,4096]{2,1,0:T(8,128)(2,1)}, u32[]{:S(2)}, u32[]{:S(2)}) async-start(bf16[16,40,4096]{2,1,0:T(8,128)(2,1)} %bitcast.58), calls=%async_computation.3 | async-start | bytes 10485760 | tf_op jit(solution)/shard_map/all_to_all | solution.py:48
  143.0 7.8 %fusion.26 = f32[640,512]{1,0:T(8,128)} fusion(bf16[640,4096]{1,0:T(8,128)(2,1)} %bitcast.7, bf16[4096,512]{1,0:T(8,128)(2,1)} %param.10), kind=kOutput, calls=%fused_computation.53 | convolution fusion | flops 2684354560 | bytes 10747904 | tf_op jit(solution)/shard_map/dot_general | solution.py:69
  150.8 6.4 %fusion.27 = f32[640,512]{1,0:T(8,128)} fusion(bf16[640,4096]{1,0:T(8,128)(2,1)} %bitcast.7, bf16[4096,512]{1,0:T(8,128)(2,1)S(1)} %copy-done.3), kind=kOutput, calls=%fused_computation.54 | convolution fusion | flops 2684354560 | bytes 10747904 | tf_op jit(solution)/shard_map/dot_general | solution.py:70
  157.2 53.1 %all-to-all-done.2 = bf16[16,40,4096]{2,1,0:T(8,128)(2,1)} async-done(((bf16[16,40,4096]{2,1,0:T(8,128)(2,1)}), bf16[16,40,4096]{2,1,0:T(8,128)(2,1)}, u32[]{:S(2)}, u32[]{:S(2)}) %all-to-all-start.2) | async-done | bytes 5242912 | tf_op jit(solution)/shard_map/all_to_all | solution.py:48
  210.3 8.0 %multiply_convert_fusion = (bf16[640,512]{1,0:T(8,128)(2,1)S(1)}, bf16[640,512]{1,0:T(8,128)(2,1)S(1)}, bf16[640,512]{1,0:T(8,128)(2,1)S(1)}) fusion(f32[640,512]{1,0:T(8,128)} %fusion.26, f32[640,512]{1,0:T(8,128)} %fusion.27, bf16[640,4096]{1,0:T(8,128)(2,1)} %bitcast.14, bf16[512,4096]{1,0:T(8,128)(2,1)} %param.12), kind=kOutput, calls=%fused_computation.9 | convolution fusion | flops 2689269760 | bytes 14024704 | tf_op jit(solution)/shard_map/dot_general | solution.py:98
  218.3 4.7 %convolution_convert_fusion = bf16[640,4096]{1,0:T(8,128)(2,1)} fusion(bf16[640,512]{1,0:T(8,128)(2,1)S(1)} %get-tuple-element.10, bf16[512,4096]{1,0:T(8,128)(2,1)S(1)} %copy-done.2), kind=kOutput, calls=%fused_computation.1 | convolution fusion | flops 2686976000 | bytes 10092544 | tf_op jit(solution)/shard_map/dot_general | solution.py:74
  223.3 4.9 %fusion.28 = f32[640,4096]{1,0:T(8,128)S(1)} fusion(bf16[640,512]{1,0:T(8,128)(2,1)S(1)} %get-tuple-element.9, bf16[4096,512]{1,0:T(8,128)(2,1)} %param.10), kind=kOutput, calls=%fused_computation.55 | convolution fusion | flops 2684354560 | bytes 15335424 | tf_op jit(solution)/shard_map/dot_general | solution.py:112
  228.2 4.8 %add_convert_fusion = bf16[640,4096]{1,0:T(8,128)(2,1)} fusion(f32[640,4096]{1,0:T(8,128)S(1)} %fusion.28, bf16[640,512]{1,0:T(8,128)(2,1)S(1)} %get-tuple-element.8, bf16[4096,512]{1,0:T(8,128)(2,1)S(1)} %copy-done.4), kind=kOutput, calls=%fused_computation | convolution fusion | flops 2689597440 | bytes 20578304 | tf_op jit(solution)/shard_map/dot_general | solution.py:115
  233.0 7.5 %convolution_convert_fusion.1 = bf16[512,4096]{1,0:T(8,128)(2,1)} fusion(bf16[640,512]{1,0:T(8,128)(2,1)S(1)} %get-tuple-element.10, bf16[640,4096]{1,0:T(8,128)(2,1)} %bitcast.14), kind=kOutput, calls=%fused_computation.2 | convolution fusion | flops 2686451712 | bytes 10092544 | tf_op jit(solution)/shard_map/dot_general | solution.py:109
  240.5 7.5 %convolution_convert_fusion.2 = bf16[4096,512]{1,0:T(8,128)(2,1)} fusion(bf16[640,4096]{1,0:T(8,128)(2,1)} %bitcast.7, bf16[640,512]{1,0:T(8,128)(2,1)S(1)} %get-tuple-element.8), kind=kOutput, calls=%fused_computation.3 | convolution fusion | flops 2686451712 | bytes 10092544 | tf_op jit(solution)/shard_map/dot_general | solution.py:106
  248.0 26.8 %reduce-scatter.3.cloned.1.call-done = bf16[640,512]{1,0:T(8,128)(2,1)} async-done(((bf16[640,4096]{1,0:T(8,128)(2,1)}), bf16[640,512]{1,0:T(8,128)(2,1)}) %reduce-scatter.3.cloned.1.call-update) | async-done | bytes 655376 | tf_op jit(solution)/shard_map/reduce_scatter | solution.py:54
  274.8 7.5 %all-to-all-start.1 = ((bf16[16,40,512]{2,1,0:T(8,128)(2,1)}), bf16[16,40,512]{2,1,0:T(8,128)(2,1)S(1)}, u32[]{:S(2)}, u32[]{:S(2)}) async-start(bf16[16,40,512]{2,1,0:T(8,128)(2,1)} %bitcast.65), calls=%async_computation.2 | async-start | bytes 1310720 | tf_op jit(solution)/shard_map/all_to_all | solution.py:57
  282.3 7.6 %convolution_convert_fusion.3 = bf16[4096,512]{1,0:T(8,128)(2,1)} fusion(bf16[640,4096]{1,0:T(8,128)(2,1)} %bitcast.7, bf16[640,512]{1,0:T(8,128)(2,1)S(1)} %get-tuple-element.9), kind=kOutput, calls=%fused_computation.4 | convolution fusion | flops 2686451712 | bytes 10092544 | tf_op jit(solution)/shard_map/dot_general | solution.py:103
  289.9 26.6 %reduce-scatter.5.cloned.1.call-done = bf16[640,512]{1,0:T(8,128)(2,1)} async-done(((bf16[640,4096]{1,0:T(8,128)(2,1)}), bf16[640,512]{1,0:T(8,128)(2,1)}) %reduce-scatter.5.cloned.1.call-update) | async-done | bytes 655376 | tf_op jit(solution)/shard_map/reduce_scatter | solution.py:54
  316.5 7.5 %all-to-all-start.3 = ((bf16[16,40,512]{2,1,0:T(8,128)(2,1)}), bf16[16,40,512]{2,1,0:T(8,128)(2,1)S(1)}, u32[]{:S(2)}, u32[]{:S(2)}) async-start(bf16[16,40,512]{2,1,0:T(8,128)(2,1)} %bitcast.64), calls=%async_computation.5 | async-start | bytes 1310720 | tf_op jit(solution)/shard_map/all_to_all | solution.py:57
  325.7 13.9 %psum.7 = f32[128,2]{0,1:T(2,128)} all-reduce(f32[128,2]{0,1:T(2,128)S(1)} %pad_maximum_fusion), channel_id=1, replica_groups=mesh['dp'=16,'fsdp'=8] {'fsdp'}, use_global_device_ids=true, to_apply=%region_9.10 | all-reduce | flops 256 | bytes 2048 | tf_op jit(solution)/shard_map/psum | solution.py:96
  (40 shorter events, 7.8 us)
Async XLA Ops:
  7.2 28.3 %all-gather.3.cloned.1.call-start = ((), (), s32[]{:S(2)}) async-start(), calls=%async_computation.6 | async-start | bytes 1179648 | tf_op jit(solution)/shard_map/all_gather | solution.py:47
  40.6 8.3 %copy-start.1 = (f32[128,2]{0,1:T(2,128)S(1)}, f32[128,2]{0,1:T(2,128)}, u32[]{:S(2)}) copy-start(f32[128,2]{0,1:T(2,128)} %param.9) | copy-start | bytes 3076
  40.6 75.1 %all-to-all-start = ((bf16[16,40,4096]{2,1,0:T(8,128)(2,1)}), bf16[16,40,4096]{2,1,0:T(8,128)(2,1)}, u32[]{:S(2)}, u32[]{:S(2)}) async-start(bf16[16,40,4096]{2,1,0:T(8,128)(2,1)} %bitcast.57), calls=%async_computation | async-start | bytes 10485760 | tf_op jit(solution)/shard_map/all_to_all | solution.py:48
  48.2 25.6 %all-gather.5.cloned.1.call-start = ((), (), s32[]{:S(2)}) async-start(), calls=%async_computation.8 | async-start | bytes 1179648 | tf_op jit(solution)/shard_map/all_gather | solution.py:47
  118.7 91.6 %all-to-all-start.2 = ((bf16[16,40,4096]{2,1,0:T(8,128)(2,1)}), bf16[16,40,4096]{2,1,0:T(8,128)(2,1)}, u32[]{:S(2)}, u32[]{:S(2)}) async-start(bf16[16,40,4096]{2,1,0:T(8,128)(2,1)} %bitcast.58), calls=%async_computation.3 | async-start | bytes 10485760 | tf_op jit(solution)/shard_map/all_to_all | solution.py:48
  142.7 132.1 %reduce-scatter.3.cloned.1.call-start = ((), (), s32[]{:S(2)}) async-start(), calls=%async_computation.7 | async-start | bytes 5898240 | tf_op jit(solution)/shard_map/reduce_scatter | solution.py:54
  142.9 7.8 %copy-start.3 = (bf16[4096,512]{1,0:T(8,128)(2,1)S(1)}, bf16[4096,512]{1,0:T(8,128)(2,1)}, u32[]{:S(2)}) copy-start(bf16[4096,512]{1,0:T(8,128)(2,1)} %param.11) | copy-start | bytes 12582916
  210.3 8.0 %copy-start.2 = (bf16[512,4096]{1,0:T(8,128)(2,1)S(1)}, bf16[512,4096]{1,0:T(8,128)(2,1)}, u32[]{:S(2)}) copy-start(bf16[512,4096]{1,0:T(8,128)(2,1)} %param.12) | copy-start | bytes 12582916
  223.0 93.5 %reduce-scatter.5.cloned.1.call-start = ((), (), s32[]{:S(2)}) async-start(), calls=%async_computation.9 | async-start | bytes 5898240 | tf_op jit(solution)/shard_map/reduce_scatter | solution.py:54
  223.3 4.9 %copy-start.4 = (bf16[4096,512]{1,0:T(8,128)(2,1)S(1)}, bf16[4096,512]{1,0:T(8,128)(2,1)}, u32[]{:S(2)}) copy-start(bf16[4096,512]{1,0:T(8,128)(2,1)} %param.11) | copy-start | bytes 12582916
  274.8 41.7 %all-to-all-start.1 = ((bf16[16,40,512]{2,1,0:T(8,128)(2,1)}), bf16[16,40,512]{2,1,0:T(8,128)(2,1)S(1)}, u32[]{:S(2)}, u32[]{:S(2)}) async-start(bf16[16,40,512]{2,1,0:T(8,128)(2,1)} %bitcast.65), calls=%async_computation.2 | async-start | bytes 1310720 | tf_op jit(solution)/shard_map/all_to_all | solution.py:57
  282.2 42.3 %copy-start = (bf16[128,512]{1,0:T(8,128)(2,1)S(1)}, bf16[128,512]{1,0:T(8,128)(2,1)}, u32[]{:S(2)}) copy-start(bf16[128,512]{1,0:T(8,128)(2,1)} %param.13) | copy-start | bytes 393220
  316.5 23.1 %all-to-all-start.3 = ((bf16[16,40,512]{2,1,0:T(8,128)(2,1)}), bf16[16,40,512]{2,1,0:T(8,128)(2,1)S(1)}, u32[]{:S(2)}, u32[]{:S(2)}) async-start(bf16[16,40,512]{2,1,0:T(8,128)(2,1)} %bitcast.64), calls=%async_computation.5 | async-start | bytes 1310720 | tf_op jit(solution)/shard_map/all_to_all | solution.py:57
Sparse Core Ops, SparseCore 0:
  9.7 25.7 all-gather.2
  50.7 23.0 all-gather.4
  223.1 51.6 reduce-scatter.2
  277.0 39.3 reduce-scatter.4
where the time goes:
time: 348 us; the launch traced here: 347 us
  waiting for transfers between devices  196 us (56%)
  matrix products  67.6 us (19%)
  starting transfers between devices  47 us (14%)
  blocking collectives  13.9 us (4%)
  between operations  13.9 us (4%)
  local copies, waits for them, and re-layouts  7.52 us (2%)
    all_to_all x2, waiting for transfers between devices, to_expert_layout(): lax.all_to_all(place_rows(joined, scaled), 'dp', split_axis=0, concat_axi...  91.5 us
    reduce_scatter x2, waiting for transfers between devices, to_token_layout(): lax.psum_scatter(partial_value.astype(jnp.bfloat16), 'fsdp', scatter_dime...  53.4 us
    all_gather x2, waiting for transfers between devices, to_expert_layout(): joined = lax.all_gather(source, 'fsdp', axis=1, tiled=True)  49.5 us
    all_to_all x2, starting transfers between devices, to_expert_layout(): lax.all_to_all(place_rows(joined, scaled), 'dp', split_axis=0, concat_axi...  31.5 us
    all_to_all x2, starting transfers between devices, to_token_layout(): lax.all_to_all(shares.reshape(dp_count, CAP, shares.shape[1]).astype(jnp....  15 us
    psum x1, blocking collectives, local(): prob_grad = lax.psum(prob_terms, 'fsdp')  13.9 us
    dot_general x1, matrix products, local(): lax.dot_general(grad_rows, w_down, back_dims, preferred_element_type=jnp....  7.96 us
    dot_general x1, matrix products, local(): gate_proj = jnp.dot(expert_rows, w_gate, preferred_element_type=jnp.float32)  7.81 us
  transfers between devices with their start and end apart: 8, of which 6 were waited for; matrix products, arithmetic and copies ran while one was open for 16% of the time, Pallas kernels for 0%

commit v1 on v0

--- a/solution.py
+++ b/solution.py
@@ -5,6 +5,12 @@
 
 E = 8
 CAP = 40
+
+
+def in_order(parts, dim):
+    parts = jnp.moveaxis(parts, 0, dim)
+    dims = parts.shape
+    return parts.reshape(*dims[:dim], dims[dim] * dims[dim + 1], *dims[dim + 2 :])
 
 
 def local(tokens, expert_ids, route_probs, w_gate, w_up, w_down, out_grad):
@@ -44,7 +50,19 @@
         return jnp.repeat(placed, groups, axis=0)
 
     def to_expert_layout(source, scaled):
-        joined = lax.all_gather(source, "fsdp", axis=1, tiled=True)
+        size = lax.axis_size("fsdp")
+        pairs = [(i, (i + 1) % size) for i in range(size)]
+        back = [(b, a) for a, b in pairs]
+        lower, upper = ([], [])
+        for lap in range(size - 1):
+            if lap % 2 == 0:
+                lower.append(lax.ppermute(lower[-1] if lower else source, "fsdp", pairs))
+            else:
+                upper.append(lax.ppermute(upper[-1] if upper else source, "fsdp", back))
+        blocks = jnp.stack([*lower[::-1], source, *upper])
+        shift = lax.axis_index("fsdp") - len(lower)
+        blocks = blocks[(jnp.arange(size) - shift) % size]
+        joined = in_order(blocks, 1)
         arrived = lax.all_to_all(
             place_rows(joined, scaled), "dp", split_axis=0, concat_axis=0, tiled=True
         )

time: 348 us -> 350 us (level)
  waiting for transfers between devices: 196 us -> 187 us
  local copies, waits for them, and re-layouts: 7.52 us -> 11.8 us
  starting transfers between devices: 47 us -> 50.9 us
    all_gather x2 -> x0, waiting for transfers between devices: 49.5 us -> none  [to_expert_layout(): joined = lax.all_gather(source, 'fsdp', axis=1, tiled=True)]
    reduce_scatter x2, waiting for transfers between devices: 53.4 us -> 79.2 us  [to_token_layout(): lax.psum_scatter(partial_value.astype(jnp.bfloat16), 'fsdp', scatter_dime...]
    ppermute x0 -> x14, waiting for transfers between devices: none -> 23.9 us  [the longest x8 23.1 us: to_expert_layout(): lower.append(lax.ppermute(lower[-1] if lower else source, 'fsdp', pairs))]
    ppermute x0 -> x14, starting transfers between devices: none -> 18.7 us  [the longest x6 18.6 us: to_expert_layout(): upper.append(lax.ppermute(upper[-1] if upper else source, 'fsdp', back))]
    all_to_all x2, starting transfers between devices: 31.5 us -> 17 us  [to_expert_layout(): lax.all_to_all(place_rows(joined, scaled), 'dp', split_axis=0, concat_axi...]
    all_to_all x2, waiting for transfers between devices: 91.5 us -> 77 us  [to_expert_layout(): lax.all_to_all(place_rows(joined, scaled), 'dp', split_axis=0, concat_axi...]
    all_to_all x2, waiting for transfers between devices: 0.01 us -> 6.94 us  [to_token_layout(): lax.all_to_all(shares.reshape(dp_count, CAP, shares.shape[1]).astype(jnp....]
  transfers between devices with their start and end apart: 8 -> 20, of which waited for: 6 -> 15; matrix products, arithmetic and copies ran while one was open for 16% -> 17% of each run, Pallas kernels for 0% -> 0%
where the time goes in v1:
time: 350 us; the launch traced here: 348 us
  waiting for transfers between devices  187 us (53%)
  matrix products  67.1 us (19%)
  starting transfers between devices  50.9 us (15%)
  blocking collectives  14.7 us (4%)
  between operations  14.3 us (4%)
  local copies, waits for them, and re-layouts  11.8 us (3%)
    reduce_scatter x2, waiting for transfers between devices, to_token_layout(): lax.psum_scatter(partial_value.astype(jnp.bfloat16), 'fsdp', scatter_dime...  79.2 us
    all_to_all x2, waiting for transfers between devices, to_expert_layout(): lax.all_to_all(place_rows(joined, scaled), 'dp', split_axis=0, concat_axi...  77 us
    ppermute x8, waiting for transfers between devices, to_expert_layout(): lower.append(lax.ppermute(lower[-1] if lower else source, 'fsdp', pairs))  23.1 us
    ppermute x6, starting transfers between devices, to_expert_layout(): upper.append(lax.ppermute(upper[-1] if upper else source, 'fsdp', back))  18.6 us
    all_to_all x2, starting transfers between devices, to_expert_layout(): lax.all_to_all(place_rows(joined, scaled), 'dp', split_axis=0, concat_axi...  17 us
    all_to_all x2, starting transfers between devices, to_token_layout(): lax.all_to_all(shares.reshape(dp_count, CAP, shares.shape[1]).astype(jnp....  14.8 us
    psum x1, blocking collectives, local(): prob_grad = lax.psum(prob_terms, 'fsdp')  14.7 us
    dot_general x1, matrix products, local(): lax.dot_general(grad_rows, w_down, back_dims, preferred_element_type=jnp....  7.96 us
  transfers between devices with their start and end apart: 20, of which 15 were waited for; matrix products, arithmetic and copies ran while one was open for 17% of the time, Pallas kernels for 0%

profile of v1, /device:TPU:2, one launch (start us, length us, event | category | flops | bytes accessed | tf_op | source)
XLA Modules:
  0.0 347.6 jit_solution(8184724764530881135)
XLA Ops:
  13.7 4.9 %collective-permute-done.1 = bf16[128,512]{1,0:T(8,128)(2,1)S(1)} collective-permute-done((bf16[128,512]{1,0:T(8,128)(2,1)S(1)}, bf16[128,512]{1,0:T(8,128)(2,1)S(1)}, u32[]{:S(2)}, u32[]{:S(2)}) %collective-permute-start.1) | collective-permute-done | bytes 131104 | tf_op jit(solution)/shard_map/ppermute | solution.py:59
  36.1 8.5 %all-to-all-start = ((bf16[16,40,4096]{2,1,0:T(8,128)(2,1)}), bf16[16,40,4096]{2,1,0:T(8,128)(2,1)}, u32[]{:S(2)}, u32[]{:S(2)}) async-start(bf16[16,40,4096]{2,1,0:T(8,128)(2,1)} %bitcast.95), calls=%async_computation | async-start | bytes 10485760 | tf_op jit(solution)/shard_map/all_to_all | solution.py:66
  44.6 5.6 %collective-permute-done.7 = bf16[128,512]{1,0:T(8,128)(2,1)S(1)} collective-permute-done((bf16[128,512]{1,0:T(8,128)(2,1)S(1)}, bf16[128,512]{1,0:T(8,128)(2,1)S(1)}, u32[]{:S(2)}, u32[]{:S(2)}) %collective-permute-start.7) | collective-permute-done | bytes 131104 | tf_op jit(solution)/shard_map/ppermute | solution.py:59
  55.8 3.4 collective-permute-start.12
  61.6 3.5 %collective-permute-start.13 = (bf16[128,512]{1,0:T(8,128)(2,1)S(1)}, bf16[128,512]{1,0:T(8,128)(2,1)S(1)}, u32[]{:S(2)}, u32[]{:S(2)}) collective-permute-start(bf16[128,512]{1,0:T(8,128)(2,1)S(1)} %collective-permute-done.12), channel_id=1, source_target_pairs={{1,0},{2,1},{3,2},{4,3},{5,4},{6,5},{7,6},{0,7},{9,8},{10,9},{11,1... | collective-permute-start | bytes 393224 | tf_op jit(solution)/shard_map/ppermute | solution.py:61
  69.6 4.1 %convolution_convert_fusion.5 = bf16[320,4096]{1,0:T(8,128)(2,1)S(1)} fusion(bf16[128,4096]{0,1:T(8,128)(2,1)} %bitcast.101, f32[128]{0:T(128)S(1)} %get-tuple-element.13, f32[128]{0:T(128)S(1)} %get-tuple-element.12, s32[128]{0:T(128)S(1)} %get-tuple-element.15, s32[128]{0:T(128)S(1)} %get-tuple-element.14), kind=kOutput, calls=%fused_computation.8 | convolution fusion | flops 2014781440 | bytes 3672064 | tf_op jit(solution)/shard_map/dot_general | solution.py:38
  73.7 30.8 %all-to-all-done = bf16[16,40,4096]{2,1,0:T(8,128)(2,1)} async-done(((bf16[16,40,4096]{2,1,0:T(8,128)(2,1)}), bf16[16,40,4096]{2,1,0:T(8,128)(2,1)}, u32[]{:S(2)}, u32[]{:S(2)}) %all-to-all-start) | async-done | bytes 5242912 | tf_op jit(solution)/shard_map/all_to_all | solution.py:66
  107.6 8.5 %all-to-all-start.2 = ((bf16[16,40,4096]{2,1,0:T(8,128)(2,1)}), bf16[16,40,4096]{2,1,0:T(8,128)(2,1)}, u32[]{:S(2)}, u32[]{:S(2)}) async-start(bf16[16,40,4096]{2,1,0:T(8,128)(2,1)} %bitcast.96), calls=%async_computation.3 | async-start | bytes 10485760 | tf_op jit(solution)/shard_map/all_to_all | solution.py:66
  116.3 7.8 %fusion.29 = f32[640,512]{1,0:T(8,128)} fusion(bf16[640,4096]{1,0:T(8,128)(2,1)} %bitcast.18, bf16[4096,512]{1,0:T(8,128)(2,1)} %param.10), kind=kOutput, calls=%fused_computation.79 | convolution fusion | flops 2684354560 | bytes 10747904 | tf_op jit(solution)/shard_map/dot_general | solution.py:87
  124.2 6.4 %fusion.30 = f32[640,512]{1,0:T(8,128)} fusion(bf16[640,4096]{1,0:T(8,128)(2,1)} %bitcast.18, bf16[4096,512]{1,0:T(8,128)(2,1)S(1)} %copy-done.3), kind=kOutput, calls=%fused_computation.80 | convolution fusion | flops 2684354560 | bytes 10747904 | tf_op jit(solution)/shard_map/dot_general | solution.py:88
  130.6 46.2 %all-to-all-done.2 = bf16[16,40,4096]{2,1,0:T(8,128)(2,1)} async-done(((bf16[16,40,4096]{2,1,0:T(8,128)(2,1)}), bf16[16,40,4096]{2,1,0:T(8,128)(2,1)}, u32[]{:S(2)}, u32[]{:S(2)}) %all-to-all-start.2) | async-done | bytes 5242912 | tf_op jit(solution)/shard_map/all_to_all | solution.py:66
  176.8 8.0 %multiply_convert_fusion = (bf16[640,512]{1,0:T(8,128)(2,1)S(1)}, bf16[640,512]{1,0:T(8,128)(2,1)S(1)}, bf16[640,512]{1,0:T(8,128)(2,1)S(1)}) fusion(f32[640,512]{1,0:T(8,128)} %fusion.29, f32[640,512]{1,0:T(8,128)} %fusion.30, bf16[640,4096]{1,0:T(8,128)(2,1)} %bitcast.35, bf16[512,4096]{1,0:T(8,128)(2,1)} %param.12), kind=kOutput, calls=%fused_computation.11 | convolution fusion | flops 2689269760 | bytes 14024704 | tf_op jit(solution)/shard_map/dot_general | solution.py:116
  184.8 4.8 %convolution_convert_fusion = bf16[640,4096]{1,0:T(8,128)(2,1)} fusion(bf16[640,512]{1,0:T(8,128)(2,1)S(1)} %get-tuple-element.10, bf16[512,4096]{1,0:T(8,128)(2,1)S(1)} %copy-done.2), kind=kOutput, calls=%fused_computation.3 | convolution fusion | flops 2686976000 | bytes 10092544 | tf_op jit(solution)/shard_map/dot_general | solution.py:92
  189.9 4.9 %fusion.31 = f32[640,4096]{1,0:T(8,128)S(1)} fusion(bf16[640,512]{1,0:T(8,128)(2,1)S(1)} %get-tuple-element.9, bf16[4096,512]{1,0:T(8,128)(2,1)} %param.10), kind=kOutput, calls=%fused_computation.81 | convolution fusion | flops 2684354560 | bytes 15335424 | tf_op jit(solution)/shard_map/dot_general | solution.py:130
  194.8 4.7 %add_convert_fusion = bf16[640,4096]{1,0:T(8,128)(2,1)} fusion(f32[640,4096]{1,0:T(8,128)S(1)} %fusion.31, bf16[640,512]{1,0:T(8,128)(2,1)S(1)} %get-tuple-element.8, bf16[4096,512]{1,0:T(8,128)(2,1)S(1)} %copy-done.4), kind=kOutput, calls=%fused_computation.2 | convolution fusion | flops 2689597440 | bytes 20578304 | tf_op jit(solution)/shard_map/dot_general | solution.py:133
  199.6 7.6 %convolution_convert_fusion.3 = bf16[4096,512]{1,0:T(8,128)(2,1)} fusion(bf16[640,4096]{1,0:T(8,128)(2,1)} %bitcast.18, bf16[640,512]{1,0:T(8,128)(2,1)S(1)} %get-tuple-element.9), kind=kOutput, calls=%fused_computation.6 | convolution fusion | flops 2686451712 | bytes 10092544 | tf_op jit(solution)/shard_map/dot_general | solution.py:121
  207.1 7.5 %convolution_convert_fusion.2 = bf16[4096,512]{1,0:T(8,128)(2,1)} fusion(bf16[640,4096]{1,0:T(8,128)(2,1)} %bitcast.18, bf16[640,512]{1,0:T(8,128)(2,1)S(1)} %get-tuple-element.8), kind=kOutput, calls=%fused_computation.5 | convolution fusion | flops 2686451712 | bytes 10092544 | tf_op jit(solution)/shard_map/dot_general | solution.py:124
  214.7 52.2 %reduce-scatter.3.cloned.1.call-done = bf16[640,512]{1,0:T(8,128)(2,1)} async-done(((bf16[640,4096]{1,0:T(8,128)(2,1)}), bf16[640,512]{1,0:T(8,128)(2,1)}) %reduce-scatter.3.cloned.1.call-update) | async-done | bytes 655376 | tf_op jit(solution)/shard_map/reduce_scatter | solution.py:72
  266.9 7.4 %all-to-all-start.1 = ((bf16[16,40,512]{2,1,0:T(8,128)(2,1)}), bf16[16,40,512]{2,1,0:T(8,128)(2,1)S(1)}, u32[]{:S(2)}, u32[]{:S(2)}) async-start(bf16[16,40,512]{2,1,0:T(8,128)(2,1)} %bitcast.107), calls=%async_computation.2 | async-start | bytes 1310720 | tf_op jit(solution)/shard_map/all_to_all | solution.py:75
  274.3 7.5 %convolution_convert_fusion.1 = bf16[512,4096]{1,0:T(8,128)(2,1)} fusion(bf16[640,512]{1,0:T(8,128)(2,1)S(1)} %get-tuple-element.10, bf16[640,4096]{1,0:T(8,128)(2,1)} %bitcast.35), kind=kOutput, calls=%fused_computation.4 | convolution fusion | flops 2686451712 | bytes 10092544 | tf_op jit(solution)/shard_map/dot_general | solution.py:127
  281.8 27.0 %reduce-scatter.5.cloned.1.call-done = bf16[640,512]{1,0:T(8,128)(2,1)} async-done(((bf16[640,4096]{1,0:T(8,128)(2,1)}), bf16[640,512]{1,0:T(8,128)(2,1)}) %reduce-scatter.5.cloned.1.call-update) | async-done | bytes 655376 | tf_op jit(solution)/shard_map/reduce_scatter | solution.py:72
  308.8 7.4 %all-to-all-start.3 = ((bf16[16,40,512]{2,1,0:T(8,128)(2,1)}), bf16[16,40,512]{2,1,0:T(8,128)(2,1)S(1)}, u32[]{:S(2)}, u32[]{:S(2)}) async-start(bf16[16,40,512]{2,1,0:T(8,128)(2,1)} %bitcast.106), calls=%async_computation.5 | async-start | bytes 1310720 | tf_op jit(solution)/shard_map/all_to_all | solution.py:75
  317.9 6.9 %all-to-all-done.3 = bf16[16,40,512]{2,1,0:T(8,128)(2,1)S(1)} async-done(((bf16[16,40,512]{2,1,0:T(8,128)(2,1)}), bf16[16,40,512]{2,1,0:T(8,128)(2,1)S(1)}, u32[]{:S(2)}, u32[]{:S(2)}) %all-to-all-start.3) | async-done | bytes 655392 | tf_op jit(solution)/shard_map/all_to_all | solution.py:75
  326.0 14.7 %psum.7 = f32[128,2]{0,1:T(2,128)} all-reduce(f32[128,2]{0,1:T(2,128)S(1)} %pad_maximum_fusion), channel_id=1, replica_groups=mesh['dp'=16,'fsdp'=8] {'fsdp'}, use_global_device_ids=true, to_apply=%region_9.10 | all-reduce | flops 256 | bytes 2048 | tf_op jit(solution)/shard_map/psum | solution.py:114
  (84 shorter events, 42.9 us)
Async XLA Ops:
  7.2 5.8 %collective-permute-start = (bf16[128,512]{1,0:T(8,128)(2,1)}, bf16[128,512]{1,0:T(8,128)(2,1)S(1)}, u32[]{:S(2)}, u32[]{:S(2)}) collective-permute-start(bf16[128,512]{1,0:T(8,128)(2,1)} %param.7), channel_id=1, source_target_pairs={{0,1},{1,2},{2,3},{3,4},{4,5},{5,6},{6,7},{7,0},{8,9},{9,10},{10,1... | collective-permute-start | bytes 393224 | tf_op jit(solution)/shard_map/ppermute | solution.py:59
  7.2 11.4 %collective-permute-start.4 = (bf16[128,512]{1,0:T(8,128)(2,1)}, bf16[128,512]{1,0:T(8,128)(2,1)S(1)}, u32[]{:S(2)}, u32[]{:S(2)}) collective-permute-start(bf16[128,512]{1,0:T(8,128)(2,1)} %param.7), channel_id=1, source_target_pairs={{1,0},{2,1},{3,2},{4,3},{5,4},{6,5},{7,6},{0,7},{9,8},{10,9},{11,1... | collective-permute-start | bytes 393224 | tf_op jit(solution)/shard_map/ppermute | solution.py:61
  13.0 5.6 %collective-permute-start.1 = (bf16[128,512]{1,0:T(8,128)(2,1)S(1)}, bf16[128,512]{1,0:T(8,128)(2,1)S(1)}, u32[]{:S(2)}, u32[]{:S(2)}) collective-permute-start(bf16[128,512]{1,0:T(8,128)(2,1)S(1)} %collective-permute-done), channel_id=1, source_target_pairs={{0,1},{1,2},{2,3},{3,4},{4,5},{5,6},{6,7},{7,0},{8,9},{9,10},{10,1... | collective-permute-start | bytes 393224 | tf_op jit(solution)/shard_map/ppermute | solution.py:59
  18.6 5.6 %collective-permute-start.2 = (bf16[128,512]{1,0:T(8,128)(2,1)S(1)}, bf16[128,512]{1,0:T(8,128)(2,1)S(1)}, u32[]{:S(2)}, u32[]{:S(2)}) collective-permute-start(bf16[128,512]{1,0:T(8,128)(2,1)S(1)} %collective-permute-done.1), channel_id=1, source_target_pairs={{0,1},{1,2},{2,3},{3,4},{4,5},{5,6},{6,7},{7,0},{8,9},{9,10},{10,1... | collective-permute-start | bytes 393224 | tf_op jit(solution)/shard_map/ppermute | solution.py:59
  18.6 5.6 %collective-permute-start.5 = (bf16[128,512]{1,0:T(8,128)(2,1)S(1)}, bf16[128,512]{1,0:T(8,128)(2,1)S(1)}, u32[]{:S(2)}, u32[]{:S(2)}) collective-permute-start(bf16[128,512]{1,0:T(8,128)(2,1)S(1)} %collective-permute-done.4), channel_id=1, source_target_pairs={{1,0},{2,1},{3,2},{4,3},{5,4},{6,5},{7,6},{0,7},{9,8},{10,9},{11,1... | collective-permute-start | bytes 393224 | tf_op jit(solution)/shard_map/ppermute | solution.py:61
  24.2 5.6 %collective-permute-start.3 = (bf16[128,512]{1,0:T(8,128)(2,1)S(1)}, bf16[128,512]{1,0:T(8,128)(2,1)S(1)}, u32[]{:S(2)}, u32[]{:S(2)}) collective-permute-start(bf16[128,512]{1,0:T(8,128)(2,1)S(1)} %collective-permute-done.2), channel_id=1, source_target_pairs={{0,1},{1,2},{2,3},{3,4},{4,5},{5,6},{6,7},{7,0},{8,9},{9,10},{10,1... | collective-permute-start | bytes 393224 | tf_op jit(solution)/shard_map/ppermute | solution.py:59
  24.2 6.6 %collective-permute-start.6 = (bf16[128,512]{1,0:T(8,128)(2,1)S(1)}, bf16[128,512]{1,0:T(8,128)(2,1)S(1)}, u32[]{:S(2)}, u32[]{:S(2)}) collective-permute-start(bf16[128,512]{1,0:T(8,128)(2,1)S(1)} %collective-permute-done.5), channel_id=1, source_target_pairs={{1,0},{2,1},{3,2},{4,3},{5,4},{6,5},{7,6},{0,7},{9,8},{10,9},{11,1... | collective-permute-start | bytes 393224 | tf_op jit(solution)/shard_map/ppermute | solution.py:61
  36.1 8.5 %copy-start = (bf16[128,512]{1,0:T(8,128)(2,1)S(1)}, bf16[128,512]{1,0:T(8,128)(2,1)}, u32[]{:S(2)}) copy-start(bf16[128,512]{1,0:T(8,128)(2,1)} %param.13) | copy-start | bytes 393220
  36.1 25.3 %copy-start.1 = (f32[128,2]{0,1:T(2,128)S(1)}, f32[128,2]{0,1:T(2,128)}, u32[]{:S(2)}) copy-start(f32[128,2]{0,1:T(2,128)} %param.9) | copy-start | bytes 3076
  36.1 68.5 %all-to-all-start = ((bf16[16,40,4096]{2,1,0:T(8,128)(2,1)}), bf16[16,40,4096]{2,1,0:T(8,128)(2,1)}, u32[]{:S(2)}, u32[]{:S(2)}) async-start(bf16[16,40,4096]{2,1,0:T(8,128)(2,1)} %bitcast.95), calls=%async_computation | async-start | bytes 10485760 | tf_op jit(solution)/shard_map/all_to_all | solution.py:66
  44.5 5.6 %collective-permute-start.7 = (bf16[128,512]{1,0:T(8,128)(2,1)S(1)}, bf16[128,512]{1,0:T(8,128)(2,1)S(1)}, u32[]{:S(2)}, u32[]{:S(2)}) collective-permute-start(bf16[128,512]{1,0:T(8,128)(2,1)S(1)} %copy-done), channel_id=1, source_target_pairs={{0,1},{1,2},{2,3},{3,4},{4,5},{5,6},{6,7},{7,0},{8,9},{9,10},{10,1... | collective-permute-start | bytes 393224 | tf_op jit(solution)/shard_map/ppermute | solution.py:59
  50.2 5.6 %collective-permute-start.8 = (bf16[128,512]{1,0:T(8,128)(2,1)S(1)}, bf16[128,512]{1,0:T(8,128)(2,1)S(1)}, u32[]{:S(2)}, u32[]{:S(2)}) collective-permute-start(bf16[128,512]{1,0:T(8,128)(2,1)S(1)} %collective-permute-done.7), channel_id=1, source_target_pairs={{0,1},{1,2},{2,3},{3,4},{4,5},{5,6},{6,7},{7,0},{8,9},{9,10},{10,1... | collective-permute-start | bytes 393224 | tf_op jit(solution)/shard_map/ppermute | solution.py:59
  50.2 5.6 %collective-permute-start.11 = (bf16[128,512]{1,0:T(8,128)(2,1)S(1)}, bf16[128,512]{1,0:T(8,128)(2,1)S(1)}, u32[]{:S(2)}, u32[]{:S(2)}) collective-permute-start(bf16[128,512]{1,0:T(8,128)(2,1)S(1)} %copy-done), channel_id=1, source_target_pairs={{1,0},{2,1},{3,2},{4,3},{5,4},{6,5},{7,6},{0,7},{9,8},{10,9},{11,1... | collective-permute-start | bytes 393224 | tf_op jit(solution)/shard_map/ppermute | solution.py:61
  55.8 5.6 %collective-permute-start.9 = (bf16[128,512]{1,0:T(8,128)(2,1)S(1)}, bf16[128,512]{1,0:T(8,128)(2,1)S(1)}, u32[]{:S(2)}, u32[]{:S(2)}) collective-permute-start(bf16[128,512]{1,0:T(8,128)(2,1)S(1)} %collective-permute-done.8), channel_id=1, source_target_pairs={{0,1},{1,2},{2,3},{3,4},{4,5},{5,6},{6,7},{7,0},{8,9},{9,10},{10,1... | collective-permute-start | bytes 393224 | tf_op jit(solution)/shard_map/ppermute | solution.py:59
  55.8 5.9 %collective-permute-start.12 = (bf16[128,512]{1,0:T(8,128)(2,1)S(1)}, bf16[128,512]{1,0:T(8,128)(2,1)S(1)}, u32[]{:S(2)}, u32[]{:S(2)}) collective-permute-start(bf16[128,512]{1,0:T(8,128)(2,1)S(1)} %collective-permute-done.11), channel_id=1, source_target_pairs={{1,0},{2,1},{3,2},{4,3},{5,4},{6,5},{7,6},{0,7},{9,8},{10,9},{11,1... | collective-permute-start | bytes 393224 | tf_op jit(solution)/shard_map/ppermute | solution.py:61
  61.4 5.6 %collective-permute-start.10 = (bf16[128,512]{1,0:T(8,128)(2,1)S(1)}, bf16[128,512]{1,0:T(8,128)(2,1)S(1)}, u32[]{:S(2)}, u32[]{:S(2)}) collective-permute-start(bf16[128,512]{1,0:T(8,128)(2,1)S(1)} %collective-permute-done.9), channel_id=1, source_target_pairs={{0,1},{1,2},{2,3},{3,4},{4,5},{5,6},{6,7},{7,0},{8,9},{9,10},{10,1... | collective-permute-start | bytes 393224 | tf_op jit(solution)/shard_map/ppermute | solution.py:59
  61.6 6.0 %collective-permute-start.13 = (bf16[128,512]{1,0:T(8,128)(2,1)S(1)}, bf16[128,512]{1,0:T(8,128)(2,1)S(1)}, u32[]{:S(2)}, u32[]{:S(2)}) collective-permute-start(bf16[128,512]{1,0:T(8,128)(2,1)S(1)} %collective-permute-done.12), channel_id=1, source_target_pairs={{1,0},{2,1},{3,2},{4,3},{5,4},{6,5},{7,6},{0,7},{9,8},{10,9},{11,1... | collective-permute-start | bytes 393224 | tf_op jit(solution)/shard_map/ppermute | solution.py:61
  107.6 69.3 %all-to-all-start.2 = ((bf16[16,40,4096]{2,1,0:T(8,128)(2,1)}), bf16[16,40,4096]{2,1,0:T(8,128)(2,1)}, u32[]{:S(2)}, u32[]{:S(2)}) async-start(bf16[16,40,4096]{2,1,0:T(8,128)(2,1)} %bitcast.96), calls=%async_computation.3 | async-start | bytes 10485760 | tf_op jit(solution)/shard_map/all_to_all | solution.py:66
  116.1 150.8 %reduce-scatter.3.cloned.1.call-start = ((), (), s32[]{:S(2)}) async-start(), calls=%async_computation.6 | async-start | bytes 5898240 | tf_op jit(solution)/shard_map/reduce_scatter | solution.py:72
  116.3 7.8 %copy-start.3 = (bf16[4096,512]{1,0:T(8,128)(2,1)S(1)}, bf16[4096,512]{1,0:T(8,128)(2,1)}, u32[]{:S(2)}) copy-start(bf16[4096,512]{1,0:T(8,128)(2,1)} %param.11) | copy-start | bytes 12582916
  176.8 8.0 %copy-start.2 = (bf16[512,4096]{1,0:T(8,128)(2,1)S(1)}, bf16[512,4096]{1,0:T(8,128)(2,1)}, u32[]{:S(2)}) copy-start(bf16[512,4096]{1,0:T(8,128)(2,1)} %param.12) | copy-start | bytes 12582916
  189.6 119.1 %reduce-scatter.5.cloned.1.call-start = ((), (), s32[]{:S(2)}) async-start(), calls=%async_computation.7 | async-start | bytes 5898240 | tf_op jit(solution)/shard_map/reduce_scatter | solution.py:72
  266.9 41.8 %all-to-all-start.1 = ((bf16[16,40,512]{2,1,0:T(8,128)(2,1)}), bf16[16,40,512]{2,1,0:T(8,128)(2,1)S(1)}, u32[]{:S(2)}, u32[]{:S(2)}) async-start(bf16[16,40,512]{2,1,0:T(8,128)(2,1)} %bitcast.107), calls=%async_computation.2 | async-start | bytes 1310720 | tf_op jit(solution)/shard_map/all_to_all | solution.py:75
  308.8 16.1 %all-to-all-start.3 = ((bf16[16,40,512]{2,1,0:T(8,128)(2,1)}), bf16[16,40,512]{2,1,0:T(8,128)(2,1)S(1)}, u32[]{:S(2)}, u32[]{:S(2)}) async-start(bf16[16,40,512]{2,1,0:T(8,128)(2,1)} %bitcast.106), calls=%async_computation.5 | async-start | bytes 1310720 | tf_op jit(solution)/shard_map/all_to_all | solution.py:75
  (1 other events, 5.0 us)
Sparse Core Ops, SparseCore 0:
  189.7 77.1 reduce-scatter.2
  269.3 39.3 reduce-scatter.4
